TPU v7x, 32 devices: a whole 2x2x4 slice. The times are simulated.
32 devices in a mesh: row: 16 (over z, x, core), col: 2 (over y).
Axes of the slice: x: 2, y: 2, z: 4, core: 2. Of those that a mesh axis runs over, the one named last changes fastest.
Arguments:
- slab: float32 [8192, 1024], P('row', 'col'), may hold values from -6 to 6
- leaf_v: float32 [8192, 256], P('row', 'col'), may hold values from -0.25 to 0.25
- leaf_t: float32 [4096, 256], P('row', 'col'), may hold values from -0.1875 to 0.1875
- tree_v: float32 [4096, 256], P('row', 'col'), may hold values from -0.375 to 0.375
- tree_t: float32 [4096, 256], P('row', 'col'), may hold values from -0.1875 to 0.1875
Outputs:
- updated_slab: float32 [8192, 1024], P('row', 'col')
All inputs are finite; a program needn't handle non-finite values.
Results may differ from a plain program's by a relative error of at most 0.0001.
Values sent between devices are 32-bit elements; how exact they have to be, the bound alone decides.
No kernel may reach another device: no remote copies, remote signals or barrier semaphores. Data moves between devices by JAX's collectives and lax.ppermute only.
A program may use at most 64 MiB of HBM per device.

v0:
```python
import jax
import jax.numpy as jnp
from jax import lax
from jax.sharding import PartitionSpec as P


def swapped(array, axis, bit):
    return lax.ppermute(array, axis, [(i, i ^ 1 << bit) for i in range(lax.axis_size(axis))])


def product(left, right):
    return jnp.dot(left, right, precision=lax.Precision.HIGHEST, preferred_element_type=jnp.float32)


def product_left_t(left, right):
    return lax.dot_general(
        left,
        right,
        (((0,), (0,)), ((), ())),
        precision=lax.Precision.HIGHEST,
        preferred_element_type=jnp.float32,
    )


def unit_lower(raw):
    row_ids = lax.broadcasted_iota(jnp.int32, raw.shape, 0)
    col_ids = lax.broadcasted_iota(jnp.int32, raw.shape, 1)
    diagonal = jnp.where(row_ids == col_ids, 1.0, 0.0).astype(raw.dtype)
    return jnp.where(row_ids > col_ids, raw, 0.0) + diagonal


def on_device(slab, leaf_v, leaf_t, tree_v, tree_t):
    leaf_full, leaf_tri = (
        lax.all_gather(leaf_v, "col", axis=1, tiled=True),
        lax.all_gather(leaf_t, "col", axis=1, tiled=True),
    )
    tree_full, tree_tri = (
        lax.all_gather(tree_v, "col", axis=1, tiled=True),
        lax.all_gather(tree_t, "col", axis=1, tiled=True),
    )
    width = leaf_tri.shape[0]
    leaf_vectors = unit_lower(leaf_full)
    leaf_factor = jnp.triu(leaf_tri)
    leaf_w = product_left_t(leaf_factor, product_left_t(leaf_vectors, slab))
    current = slab[:width] - product(leaf_vectors[:width], leaf_w)
    remainder = slab[width:] - product(leaf_vectors[width:], leaf_w)
    tree_vectors = jnp.triu(tree_full)
    tree_factor = jnp.triu(tree_tri)
    position = lax.axis_index("row")
    levels = lax.axis_size("row").bit_length() - 1
    for level in range(levels):
        step = 1 << level
        phase = position % (2 * step)
        is_lower = phase == 0
        is_upper = phase == step
        projected = product_left_t(tree_vectors, current)
        outgoing = jnp.where(is_upper, projected, current)
        received, partner_factor = swapped((outgoing, tree_factor), "row", level)
        merged = jnp.where(is_upper, received + projected, current + received)
        pair_factor = jnp.where(is_upper, tree_factor, partner_factor)
        update = product_left_t(pair_factor, merged)
        raised = current - product(tree_vectors, update)
        lowered = current - update
        current = jnp.where(is_upper, raised, jnp.where(is_lower, lowered, current))
    return jnp.concatenate([current, remainder], axis=0)


def solution(mesh):
    in_specs = (P("row", "col"), P("row", "col"), P("row", "col"), P("row", "col"), P("row", "col"))
    out_specs = P("row", "col")
    return jax.shard_map(
        on_device, mesh=mesh, in_specs=in_specs, out_specs=out_specs, check_vma=False
    )
```

profile of v0, /device:TPU:0, one launch (start us, length us, event | category | flops | bytes accessed | tf_op | source)
XLA Modules:
  0.0 124.4 jit_solution(8653530077791594265)
XLA Ops:
  0.0 0.0 copy-start
  0.0 10.3 %all_gather.12 = f32[512,256]{1,0:T(8,128)S(1)} all-gather(f32[512,128]{1,0:T(8,128)} %param.6), channel_id=1, replica_groups=mesh['row'=16,'col'=2] {'col'}, dimensions={1}, use_global_device_ids=true | all-gather | bytes 786432 | tf_op jit(solution)/shard_map/all_gather | solution.py:34
  10.4 0.0 copy-done
  10.4 0.0 copy-start.1
  10.4 0.0 copy-start.4
  10.4 1.1 fusion.41
  11.5 0.0 copy-done.4
  11.5 0.0 copy-start.5
  11.5 5.8 %all_gather.13 = f32[256,256]{1,0:T(8,128)S(1)} all-gather(f32[256,128]{1,0:T(8,128)S(1)} %copy-done.4), channel_id=1, replica_groups=mesh['row'=16,'col'=2] {'col'}, dimensions={1}, use_global_device_ids=true | all-gather | bytes 393216 | tf_op jit(solution)/shard_map/all_gather | solution.py:35
  17.3 0.0 copy-done.5
  17.3 5.6 %all_gather.14 = f32[256,256]{1,0:T(8,128)S(1)} all-gather(f32[256,128]{1,0:T(8,128)S(1)} %copy-done.5), channel_id=1, replica_groups=mesh['row'=16,'col'=2] {'col'}, dimensions={1}, use_global_device_ids=true | all-gather | bytes 393216 | tf_op jit(solution)/shard_map/all_gather | solution.py:38
  22.9 0.7 fusion.26
  23.6 0.0 copy-done.1
  23.6 0.6 convolution_subtract_fusion.5
  24.3 0.0 copy-start.6
  24.3 1.5 %broadcast_select_fusion = (f32[256,512]{1,0:T(8,128)}, f32[256,512]{1,0:T(8,128)S(1)}) fusion(f32[256,512]{1,0:T(8,128)S(1)} %convolution_subtract_fusion.5, pred[]{:T(512)S(6)} %eq.35, f32[256,256]{1,0:T(8,128)S(1)} %all_gather.14, s32[256]{0:T(256)S(1)} %iota_add_fusion), kind=kOutput, calls=%fused_computation.46 | convolution fusion | flops 402915328 | bytes 1836033 | tf_op jit(solution)/shard_map/dot_general | solution.py:16
  25.8 0.0 collective-permute-start.1
  25.8 0.0 copy-done.6
  25.8 6.8 %all_gather.15 = f32[256,256]{1,0:T(8,128)S(1)} all-gather(f32[256,128]{1,0:T(8,128)S(1)} %copy-done.6), channel_id=1, replica_groups=mesh['row'=16,'col'=2] {'col'}, dimensions={1}, use_global_device_ids=true | all-gather | bytes 393216 | tf_op jit(solution)/shard_map/all_gather | solution.py:39
  32.5 0.1 fusion.28
  32.6 0.1 collective-permute-start
  32.7 1.5 %collective-permute-done = f32[256,256]{1,0:T(8,128)S(1)} collective-permute-done((f32[256,256]{1,0:T(8,128)S(1)}, f32[256,256]{1,0:T(8,128)S(1)}, u32[]{:S(2)}, u32[]{:S(2)}) %collective-permute-start) | collective-permute-done | bytes 262176 | tf_op jit(solution)/shard_map/ppermute | solution.py:8
  34.2 0.0 collective-permute-done.1
  34.2 1.7 %fusion.16 = f32[256,512]{1,0:T(8,128)S(1)} fusion(f32[256,512]{1,0:T(8,128)S(1)} %convolution_subtract_fusion.5, f32[256,512]{1,0:T(8,128)} %collective-permute-done.1, f32[256,512]{1,0:T(8,128)S(1)} %get-tuple-element.6, f32[256,256]{1,0:T(8,128)S(1)} %fusion.28, f32[256,256]{1,0:T(8,128)S(1)} %collective-permute-done, pred[]{:T(512)S(6)} %eq.35), kind=kOutput, calls=%fused_computation.27 | convolution fusion | flops 403111936 | bytes 2621441 | tf_op jit(solution)/shard_map/dot_general | solution.py:16
  36.0 0.7 fusion
  36.7 1.5 %broadcast_select_fusion.1 = (f32[256,512]{1,0:T(8,128)}, f32[256,512]{1,0:T(8,128)S(1)}) fusion(f32[256,512]{1,0:T(8,128)S(1)} %fusion, pred[]{:T(512)S(6)} %eq.34, f32[256,256]{1,0:T(8,128)S(1)} %all_gather.14, s32[256]{0:T(256)S(1)} %iota_add_fusion), kind=kOutput, calls=%fused_computation.48 | convolution fusion | flops 402915328 | bytes 1836033 | tf_op jit(solution)/shard_map/dot_general | solution.py:16
  38.2 1.7 %collective-permute-start.3 = (f32[256,512]{1,0:T(8,128)}, f32[256,512]{1,0:T(8,128)}, u32[]{:S(2)}, u32[]{:S(2)}) collective-permute-start(f32[256,512]{1,0:T(8,128)} %get-tuple-element.7), channel_id=1, source_target_pairs={{0,4},{2,6},{4,0},{6,2},{8,12},{10,14},{12,8},{14,10},{16,20},{18,... | collective-permute-start | bytes 1572872 | tf_op jit(solution)/shard_map/ppermute | solution.py:8
  39.8 0.4 collective-permute-start.2
  40.2 17.8 %collective-permute-done.2 = f32[256,256]{1,0:T(8,128)S(1)} collective-permute-done((f32[256,256]{1,0:T(8,128)S(1)}, f32[256,256]{1,0:T(8,128)S(1)}, u32[]{:S(2)}, u32[]{:S(2)}) %collective-permute-start.2) | collective-permute-done | bytes 262176 | tf_op jit(solution)/shard_map/ppermute | solution.py:8
  58.0 0.0 collective-permute-done.3
  58.0 1.7 %fusion.12 = f32[256,512]{1,0:T(8,128)S(1)} fusion(f32[256,512]{1,0:T(8,128)S(1)} %fusion, f32[256,512]{1,0:T(8,128)} %collective-permute-done.3, f32[256,512]{1,0:T(8,128)S(1)} %get-tuple-element.8, f32[256,256]{1,0:T(8,128)S(1)} %fusion.28, f32[256,256]{1,0:T(8,128)S(1)} %collective-permute-done.2, pred[]{:T(512)S(6)} %eq.34), kind=kOutput, calls=%fused_computation.23 | convolution fusion | flops 403111936 | bytes 2621441 | tf_op jit(solution)/shard_map/dot_general | solution.py:16
  59.7 0.7 fusion.1
  60.4 1.5 %broadcast_select_fusion.2 = (f32[256,512]{1,0:T(8,128)}, f32[256,512]{1,0:T(8,128)S(1)}) fusion(f32[256,512]{1,0:T(8,128)S(1)} %fusion.1, pred[]{:T(512)S(6)} %eq.33, f32[256,256]{1,0:T(8,128)S(1)} %all_gather.14, s32[256]{0:T(256)S(1)} %iota_add_fusion), kind=kOutput, calls=%fused_computation.50 | convolution fusion | flops 402915328 | bytes 1836033 | tf_op jit(solution)/shard_map/dot_general | solution.py:16
  61.9 1.8 %collective-permute-start.5 = (f32[256,512]{1,0:T(8,128)}, f32[256,512]{1,0:T(8,128)}, u32[]{:S(2)}, u32[]{:S(2)}) collective-permute-start(f32[256,512]{1,0:T(8,128)} %get-tuple-element.9), channel_id=1, source_target_pairs={{0,8},{2,10},{4,12},{6,14},{8,0},{10,2},{12,4},{14,6},{16,24},{18,... | collective-permute-start | bytes 1572872 | tf_op jit(solution)/shard_map/ppermute | solution.py:8
  63.7 0.3 collective-permute-start.4
  63.9 17.0 %collective-permute-done.4 = f32[256,256]{1,0:T(8,128)S(1)} collective-permute-done((f32[256,256]{1,0:T(8,128)S(1)}, f32[256,256]{1,0:T(8,128)S(1)}, u32[]{:S(2)}, u32[]{:S(2)}) %collective-permute-start.4) | collective-permute-done | bytes 262176 | tf_op jit(solution)/shard_map/ppermute | solution.py:8
  80.9 0.0 collective-permute-done.5
  80.9 1.7 %fusion.8 = f32[256,512]{1,0:T(8,128)S(1)} fusion(f32[256,512]{1,0:T(8,128)S(1)} %fusion.1, f32[256,512]{1,0:T(8,128)} %collective-permute-done.5, f32[256,512]{1,0:T(8,128)S(1)} %get-tuple-element.10, f32[256,256]{1,0:T(8,128)S(1)} %fusion.28, f32[256,256]{1,0:T(8,128)S(1)} %collective-permute-done.4, pred[]{:T(512)S(6)} %eq.33), kind=kOutput, calls=%fused_computation.19 | convolution fusion | flops 403111936 | bytes 2621441 | tf_op jit(solution)/shard_map/dot_general | solution.py:16
  82.6 0.7 fusion.2
  83.3 0.0 copy-start.2
  83.3 1.7 %broadcast_select_fusion.3 = (f32[256,512]{1,0:T(8,128)}, f32[256,512]{1,0:T(8,128)}) fusion(f32[256,512]{1,0:T(8,128)S(1)} %fusion.2, pred[]{:T(512)S(6)} %eq.32, f32[256,256]{1,0:T(8,128)S(1)} %all_gather.14, s32[256]{0:T(256)S(1)} %iota_add_fusion), kind=kOutput, calls=%fused_computation.52 | convolution fusion | flops 402915328 | bytes 1836033 | tf_op jit(solution)/shard_map/dot_general | solution.py:16
  85.0 2.8 %collective-permute-start.7 = (f32[256,512]{1,0:T(8,128)}, f32[256,512]{1,0:T(8,128)}, u32[]{:S(2)}, u32[]{:S(2)}) collective-permute-start(f32[256,512]{1,0:T(8,128)} %get-tuple-element.11), channel_id=1, source_target_pairs={{0,16},{2,18},{4,20},{6,22},{8,24},{10,26},{12,28},{14,30},{16,0},... | collective-permute-start | bytes 1572872 | tf_op jit(solution)/shard_map/ppermute | solution.py:8
  87.8 0.2 collective-permute-start.6
  87.9 0.0 copy-done.2
  87.9 0.0 copy-start.3
  87.9 0.6 convolution_subtract_fusion
  88.6 32.4 %collective-permute-done.6 = f32[256,256]{1,0:T(8,128)S(1)} collective-permute-done((f32[256,256]{1,0:T(8,128)S(1)}, f32[256,256]{1,0:T(8,128)S(1)}, u32[]{:S(2)}, u32[]{:S(2)}) %collective-permute-start.6) | collective-permute-done | bytes 262176 | tf_op jit(solution)/shard_map/ppermute | solution.py:8
  120.9 0.0 collective-permute-done.7
  120.9 0.0 copy-done.3
  120.9 1.7 %fusion.4 = f32[256,512]{1,0:T(8,128)S(1)} fusion(f32[256,512]{1,0:T(8,128)S(1)} %fusion.2, f32[256,512]{1,0:T(8,128)} %collective-permute-done.7, f32[256,512]{1,0:T(8,128)S(1)} %copy-done.3, f32[256,256]{1,0:T(8,128)S(1)} %fusion.28, f32[256,256]{1,0:T(8,128)S(1)} %collective-permute-done.6, pred[]{:T(512)S(6)} %eq.32), kind=kOutput, calls=%fused_computation.15 | convolution fusion | flops 403111936 | bytes 2621441 | tf_op jit(solution)/shard_map/dot_general | solution.py:16
  122.7 0.7 fusion.3
  123.4 1.0 pad_maximum_fusion
  (2 shorter events, 0.0 us)
Async XLA Ops:
  0.0 10.4 %copy-start = (f32[512,512]{1,0:T(8,128)S(1)}, f32[512,512]{1,0:T(8,128)}, u32[]{:S(2)}) copy-start(f32[512,512]{1,0:T(8,128)} %param.5) | copy-start | bytes 3145732
  10.4 13.2 %copy-start.1 = (f32[512,256]{1,0:T(8,128)}, f32[512,256]{1,0:T(8,128)S(1)}, u32[]{:S(2)}) copy-start(f32[512,256]{1,0:T(8,128)S(1)} %select_add_fusion) | copy-start | bytes 1572868
  10.4 1.1 copy-start.4
  11.5 5.8 %copy-start.5 = (f32[256,128]{1,0:T(8,128)S(1)}, f32[256,128]{1,0:T(8,128)}, u32[]{:S(2)}) copy-start(f32[256,128]{1,0:T(8,128)} %param.8) | copy-start | bytes 393220
  24.3 1.5 %copy-start.6 = (f32[256,128]{1,0:T(8,128)S(1)}, f32[256,128]{1,0:T(8,128)}, u32[]{:S(2)}) copy-start(f32[256,128]{1,0:T(8,128)} %param.9) | copy-start | bytes 393220
  25.8 8.5 %collective-permute-start.1 = (f32[256,512]{1,0:T(8,128)}, f32[256,512]{1,0:T(8,128)}, u32[]{:S(2)}, u32[]{:S(2)}) collective-permute-start(f32[256,512]{1,0:T(8,128)} %get-tuple-element.5), channel_id=1, source_target_pairs={{0,2},{2,0},{4,6},{6,4},{8,10},{10,8},{12,14},{14,12},{16,18},{18,... | collective-permute-start | bytes 1572872 | tf_op jit(solution)/shard_map/ppermute | solution.py:8
  32.6 1.6 %collective-permute-start = (f32[256,256]{1,0:T(8,128)S(1)}, f32[256,256]{1,0:T(8,128)S(1)}, u32[]{:S(2)}, u32[]{:S(2)}) collective-permute-start(f32[256,256]{1,0:T(8,128)S(1)} %fusion.28), channel_id=1, source_target_pairs={{0,2},{2,0},{4,6},{6,4},{8,10},{10,8},{12,14},{14,12},{16,18},{18,... | collective-permute-start | bytes 786440 | tf_op jit(solution)/shard_map/ppermute | solution.py:8
  38.2 19.8 %collective-permute-start.3 = (f32[256,512]{1,0:T(8,128)}, f32[256,512]{1,0:T(8,128)}, u32[]{:S(2)}, u32[]{:S(2)}) collective-permute-start(f32[256,512]{1,0:T(8,128)} %get-tuple-element.7), channel_id=1, source_target_pairs={{0,4},{2,6},{4,0},{6,2},{8,12},{10,14},{12,8},{14,10},{16,20},{18,... | collective-permute-start | bytes 1572872 | tf_op jit(solution)/shard_map/ppermute | solution.py:8
  39.8 18.1 %collective-permute-start.2 = (f32[256,256]{1,0:T(8,128)S(1)}, f32[256,256]{1,0:T(8,128)S(1)}, u32[]{:S(2)}, u32[]{:S(2)}) collective-permute-start(f32[256,256]{1,0:T(8,128)S(1)} %fusion.28), channel_id=1, source_target_pairs={{0,4},{2,6},{4,0},{6,2},{8,12},{10,14},{12,8},{14,10},{16,20},{18,... | collective-permute-start | bytes 786440 | tf_op jit(solution)/shard_map/ppermute | solution.py:8
  61.9 19.0 %collective-permute-start.5 = (f32[256,512]{1,0:T(8,128)}, f32[256,512]{1,0:T(8,128)}, u32[]{:S(2)}, u32[]{:S(2)}) collective-permute-start(f32[256,512]{1,0:T(8,128)} %get-tuple-element.9), channel_id=1, source_target_pairs={{0,8},{2,10},{4,12},{6,14},{8,0},{10,2},{12,4},{14,6},{16,24},{18,... | collective-permute-start | bytes 1572872 | tf_op jit(solution)/shard_map/ppermute | solution.py:8
  63.7 17.2 %collective-permute-start.4 = (f32[256,256]{1,0:T(8,128)S(1)}, f32[256,256]{1,0:T(8,128)S(1)}, u32[]{:S(2)}, u32[]{:S(2)}) collective-permute-start(f32[256,256]{1,0:T(8,128)S(1)} %fusion.28), channel_id=1, source_target_pairs={{0,8},{2,10},{4,12},{6,14},{8,0},{10,2},{12,4},{14,6},{16,24},{18,... | collective-permute-start | bytes 786440 | tf_op jit(solution)/shard_map/ppermute | solution.py:8
  83.3 4.6 %copy-start.2 = (f32[512,256]{1,0:T(8,128)S(1)}, f32[512,256]{1,0:T(8,128)}, u32[]{:S(2)}) copy-start(f32[512,256]{1,0:T(8,128)} %copy-done.1) | copy-start | bytes 1572868
  85.0 35.9 %collective-permute-start.7 = (f32[256,512]{1,0:T(8,128)}, f32[256,512]{1,0:T(8,128)}, u32[]{:S(2)}, u32[]{:S(2)}) collective-permute-start(f32[256,512]{1,0:T(8,128)} %get-tuple-element.11), channel_id=1, source_target_pairs={{0,16},{2,18},{4,20},{6,22},{8,24},{10,26},{12,28},{14,30},{16,0},... | collective-permute-start | bytes 1572872 | tf_op jit(solution)/shard_map/ppermute | solution.py:8
  87.8 33.2 %collective-permute-start.6 = (f32[256,256]{1,0:T(8,128)S(1)}, f32[256,256]{1,0:T(8,128)S(1)}, u32[]{:S(2)}, u32[]{:S(2)}) collective-permute-start(f32[256,256]{1,0:T(8,128)S(1)} %fusion.28), channel_id=1, source_target_pairs={{0,16},{2,18},{4,20},{6,22},{8,24},{10,26},{12,28},{14,30},{16,0},... | collective-permute-start | bytes 786440 | tf_op jit(solution)/shard_map/ppermute | solution.py:8
  87.9 33.0 %copy-start.3 = (f32[256,512]{1,0:T(8,128)S(1)}, f32[256,512]{1,0:T(8,128)}, u32[]{:S(2)}) copy-start(f32[256,512]{1,0:T(8,128)} %get-tuple-element.12) | copy-start | bytes 1572868
where the time goes:
time: 125 us; the launch traced here: 124 us
  waiting for transfers between devices  68.6 us (55%)
  blocking collectives  28.5 us (23%)
  matrix products  18.8 us (15%)
  starting transfers between devices  7.05 us (6%)
    ppermute x8, waiting for transfers between devices, swapped(): lax.ppermute(array, axis, [(i, i ^ 1 << bit) for i in range(lax.axis_size...  68.6 us
    dot_general x10, matrix products, product_left_t(): lax.dot_general(left, right, (((0,), (0,)), ((), ())), precision=lax.Prec...  14.9 us
    all_gather x1, blocking collectives, on_device(): lax.all_gather(leaf_v, 'col', axis=1, tiled=True)  10.3 us
    ppermute x8, starting transfers between devices, swapped(): lax.ppermute(array, axis, [(i, i ^ 1 << bit) for i in range(lax.axis_size...  7.05 us
    all_gather x1, blocking collectives, on_device(): lax.all_gather(tree_t, 'col', axis=1, tiled=True)  6.75 us
    all_gather x1, blocking collectives, on_device(): lax.all_gather(leaf_t, 'col', axis=1, tiled=True)  5.78 us
    all_gather x1, blocking collectives, on_device(): lax.all_gather(tree_v, 'col', axis=1, tiled=True)  5.63 us
    dot_general x6, matrix products, product(): jnp.dot(left, right, precision=lax.Precision.HIGHEST, preferred_element_t...  3.94 us
  transfers between devices with their start and end apart: 8, of which 4 were waited for; matrix products, arithmetic and copies ran while one was open for 1% of the time, Pallas kernels for 0%

commit v1 on v0

--- a/solution.py
+++ b/solution.py
@@ -2,6 +2,19 @@
 import jax.numpy as jnp
 from jax import lax
 from jax.sharding import PartitionSpec as P
+
+
+def group_views(x_in):
+    built = lax.axis_index("col")
+    u1 = lax.axis_size("col")
+    even, s_next, before = (u1, built, x_in.shape[1])
+    opened, block_now = (x_in, 1)
+    while block_now < even:
+        part_next = tuple(((nth, (nth - block_now) % even) for nth in range(even)))
+        state_next = lax.ppermute(opened, "col", part_next)
+        opened = jnp.concatenate([opened, state_next], 1)
+        block_now = 2 * block_now
+    return jnp.roll(opened, s_next * before, 1)
 
 
 def swapped(array, axis, bit):
@@ -30,10 +43,7 @@
 
 
 def on_device(slab, leaf_v, leaf_t, tree_v, tree_t):
-    leaf_full, leaf_tri = (
-        lax.all_gather(leaf_v, "col", axis=1, tiled=True),
-        lax.all_gather(leaf_t, "col", axis=1, tiled=True),
-    )
+    leaf_full, leaf_tri = (group_views(leaf_v), lax.all_gather(leaf_t, "col", axis=1, tiled=True))
     tree_full, tree_tri = (
         lax.all_gather(tree_v, "col", axis=1, tiled=True),
         lax.all_gather(tree_t, "col", axis=1, tiled=True),

time: 125 us -> 118 us (0.944)
  blocking collectives: 28.5 us -> 21.9 us
  matrix products: 18.8 us -> 15.5 us
  starting transfers between devices: 7.05 us -> 10 us
    all_gather x1 -> x0, blocking collectives: 10.3 us -> none  [on_device(): lax.all_gather(leaf_v, 'col', axis=1, tiled=True)]
    dot_general x10, matrix products: 14.9 us -> 10.5 us  [product_left_t(): lax.dot_general(left, right, (((0,), (0,)), ((), ())), precision=lax.Prec...]
    all_gather x1, blocking collectives: 5.78 us -> 9.32 us  [on_device(): lax.all_gather(leaf_t, 'col', axis=1, tiled=True)]
    ppermute x0 -> x1, starting transfers between devices: none -> 2.97 us  [group_views(): state_next = lax.ppermute(opened, 'col', part_next)]
  transfers between devices with their start and end apart: 8 -> 9, of which waited for: 4 -> 4; matrix products, arithmetic and copies ran while one was open for 1% -> 1% of each run, Pallas kernels for 0% -> 0%
where the time goes in v1:
time: 118 us; the launch traced here: 117 us
  waiting for transfers between devices  67.6 us (57%)
  blocking collectives  21.9 us (19%)
  matrix products  15.5 us (13%)
  starting transfers between devices  10 us (8%)
  other arithmetic  2.22 us (2%)
    ppermute x8, waiting for transfers between devices, swapped(): lax.ppermute(array, axis, [(i, i ^ 1 << bit) for i in range(lax.axis_size...  67.6 us
    dot_general x10, matrix products, product_left_t(): lax.dot_general(left, right, (((0,), (0,)), ((), ())), precision=lax.Prec...  10.5 us
    all_gather x1, blocking collectives, on_device(): lax.all_gather(leaf_t, 'col', axis=1, tiled=True)  9.32 us
    ppermute x8, starting transfers between devices, swapped(): lax.ppermute(array, axis, [(i, i ^ 1 << bit) for i in range(lax.axis_size...  7.05 us
    all_gather x1, blocking collectives, on_device(): lax.all_gather(tree_t, 'col', axis=1, tiled=True)  6.75 us
    all_gather x1, blocking collectives, on_device(): lax.all_gather(tree_v, 'col', axis=1, tiled=True)  5.84 us
    dot_general x6, matrix products, product(): jnp.dot(left, right, precision=lax.Precision.HIGHEST, preferred_element_t...  4.98 us
    ppermute x1, starting transfers between devices, group_views(): state_next = lax.ppermute(opened, 'col', part_next)  2.97 us
  transfers between devices with their start and end apart: 9, of which 4 were waited for; matrix products, arithmetic and copies ran while one was open for 1% of the time, Pallas kernels for 0%

profile of v1, /device:TPU:0, one launch (start us, length us, event | category | flops | bytes accessed | tf_op | source)
XLA Modules:
  0.0 117.4 jit_solution(7074838370967924762)
XLA Ops:
  0.0 0.0 copy-start
  0.0 3.0 %collective-permute-start = (f32[512,128]{1,0:T(8,128)}, f32[512,128]{1,0:T(8,128)S(1)}, u32[]{:S(2)}, u32[]{:S(2)}) collective-permute-start(f32[512,128]{1,0:T(8,128)} %param.6), channel_id=1, source_target_pairs={{0,1},{1,0},{2,3},{3,2},{4,5},{5,4},{6,7},{7,6},{8,9},{9,8},{10,11... | collective-permute-start | bytes 786440 | tf_op jit(solution)/shard_map/ppermute | solution.py:14
  3.0 9.3 %all_gather.9 = f32[256,256]{1,0:T(8,128)S(1)} all-gather(f32[256,128]{1,0:T(8,128)} %param.7), channel_id=1, replica_groups=mesh['row'=16,'col'=2] {'col'}, dimensions={1}, use_global_device_ids=true | all-gather | bytes 393216 | tf_op jit(solution)/shard_map/all_gather | solution.py:46
  12.3 5.8 %all_gather.10 = f32[256,256]{1,0:T(8,128)S(1)} all-gather(f32[256,128]{1,0:T(8,128)} %param.8), channel_id=1, replica_groups=mesh['row'=16,'col'=2] {'col'}, dimensions={1}, use_global_device_ids=true | all-gather | bytes 393216 | tf_op jit(solution)/shard_map/all_gather | solution.py:48
  18.1 0.0 collective-permute-done
  18.1 1.1 fusion.8
  19.2 0.0 copy-done
  19.2 1.1 fusion.66
  20.3 0.7 fusion.31
  21.0 0.6 convolution_subtract_fusion.5
  21.6 0.0 copy-start.1
  21.6 1.5 %broadcast_select_fusion = (f32[256,512]{1,0:T(8,128)}, f32[256,512]{1,0:T(8,128)S(1)}) fusion(f32[256,512]{1,0:T(8,128)S(1)} %convolution_subtract_fusion.5, pred[]{:T(512)S(6)} %eq.38, f32[256,256]{1,0:T(8,128)S(1)} %all_gather.10, s32[256]{0:T(256)S(1)} %iota_add_fusion), kind=kOutput, calls=%fused_computation.54 | convolution fusion | flops 402915328 | bytes 1836033 | tf_op jit(solution)/shard_map/dot_general | solution.py:29
  23.1 0.0 collective-permute-start.2
  23.1 0.0 copy-done.1
  23.2 6.8 %all_gather.11 = f32[256,256]{1,0:T(8,128)S(1)} all-gather(f32[256,128]{1,0:T(8,128)S(1)} %copy-done.1), channel_id=1, replica_groups=mesh['row'=16,'col'=2] {'col'}, dimensions={1}, use_global_device_ids=true | all-gather | bytes 393216 | tf_op jit(solution)/shard_map/all_gather | solution.py:49
  29.9 0.1 fusion.33
  30.0 0.1 collective-permute-start.1
  30.1 1.5 %collective-permute-done.1 = f32[256,256]{1,0:T(8,128)S(1)} collective-permute-done((f32[256,256]{1,0:T(8,128)S(1)}, f32[256,256]{1,0:T(8,128)S(1)}, u32[]{:S(2)}, u32[]{:S(2)}) %collective-permute-start.1) | collective-permute-done | bytes 262176 | tf_op jit(solution)/shard_map/ppermute | solution.py:21
  31.6 0.0 collective-permute-done.2
  31.6 0.7 fusion.21
  32.3 0.7 fusion
  33.0 1.5 %broadcast_select_fusion.1 = (f32[256,512]{1,0:T(8,128)}, f32[256,512]{1,0:T(8,128)S(1)}) fusion(f32[256,512]{1,0:T(8,128)S(1)} %fusion, pred[]{:T(512)S(6)} %eq.37, f32[256,256]{1,0:T(8,128)S(1)} %all_gather.10, s32[256]{0:T(256)S(1)} %iota_add_fusion), kind=kOutput, calls=%fused_computation.56 | convolution fusion | flops 402915328 | bytes 1836033 | tf_op jit(solution)/shard_map/dot_general | solution.py:29
  34.5 1.7 %collective-permute-start.4 = (f32[256,512]{1,0:T(8,128)}, f32[256,512]{1,0:T(8,128)S(1)}, u32[]{:S(2)}, u32[]{:S(2)}) collective-permute-start(f32[256,512]{1,0:T(8,128)} %get-tuple-element.7), channel_id=1, source_target_pairs={{0,4},{2,6},{4,0},{6,2},{8,12},{10,14},{12,8},{14,10},{16,20},{18,... | collective-permute-start | bytes 1572872 | tf_op jit(solution)/shard_map/ppermute | solution.py:21
  36.2 0.3 collective-permute-start.3
  36.5 17.8 %collective-permute-done.3 = f32[256,256]{1,0:T(8,128)S(1)} collective-permute-done((f32[256,256]{1,0:T(8,128)S(1)}, f32[256,256]{1,0:T(8,128)S(1)}, u32[]{:S(2)}, u32[]{:S(2)}) %collective-permute-start.3) | collective-permute-done | bytes 262176 | tf_op jit(solution)/shard_map/ppermute | solution.py:21
  54.3 0.0 collective-permute-done.4
  54.3 0.7 fusion.17
  55.0 0.7 fusion.1
  55.7 1.5 %broadcast_select_fusion.2 = (f32[256,512]{1,0:T(8,128)}, f32[256,512]{1,0:T(8,128)S(1)}) fusion(f32[256,512]{1,0:T(8,128)S(1)} %fusion.1, pred[]{:T(512)S(6)} %eq.36, f32[256,256]{1,0:T(8,128)S(1)} %all_gather.10, s32[256]{0:T(256)S(1)} %iota_add_fusion), kind=kOutput, calls=%fused_computation.58 | convolution fusion | flops 402915328 | bytes 1836033 | tf_op jit(solution)/shard_map/dot_general | solution.py:29
  57.2 1.8 %collective-permute-start.6 = (f32[256,512]{1,0:T(8,128)}, f32[256,512]{1,0:T(8,128)S(1)}, u32[]{:S(2)}, u32[]{:S(2)}) collective-permute-start(f32[256,512]{1,0:T(8,128)} %get-tuple-element.9), channel_id=1, source_target_pairs={{0,8},{2,10},{4,12},{6,14},{8,0},{10,2},{12,4},{14,6},{16,24},{18,... | collective-permute-start | bytes 1572872 | tf_op jit(solution)/shard_map/ppermute | solution.py:21
  59.0 0.2 collective-permute-start.5
  59.2 17.0 %collective-permute-done.5 = f32[256,256]{1,0:T(8,128)S(1)} collective-permute-done((f32[256,256]{1,0:T(8,128)S(1)}, f32[256,256]{1,0:T(8,128)S(1)}, u32[]{:S(2)}, u32[]{:S(2)}) %collective-permute-start.5) | collective-permute-done | bytes 262176 | tf_op jit(solution)/shard_map/ppermute | solution.py:21
  76.2 0.0 collective-permute-done.6
  76.2 0.7 fusion.13
  76.9 0.7 fusion.2
  77.6 1.5 %broadcast_select_fusion.3 = (f32[256,512]{1,0:T(8,128)}, f32[256,512]{1,0:T(8,128)S(1)}) fusion(f32[256,512]{1,0:T(8,128)S(1)} %fusion.2, pred[]{:T(512)S(6)} %eq.35, f32[256,256]{1,0:T(8,128)S(1)} %all_gather.10, s32[256]{0:T(256)S(1)} %iota_add_fusion), kind=kOutput, calls=%fused_computation.60 | convolution fusion | flops 402915328 | bytes 1836033 | tf_op jit(solution)/shard_map/dot_general | solution.py:29
  79.1 2.8 %collective-permute-start.8 = (f32[256,512]{1,0:T(8,128)}, f32[256,512]{1,0:T(8,128)S(1)}, u32[]{:S(2)}, u32[]{:S(2)}) collective-permute-start(f32[256,512]{1,0:T(8,128)} %get-tuple-element.11), channel_id=1, source_target_pairs={{0,16},{2,18},{4,20},{6,22},{8,24},{10,26},{12,28},{14,30},{16,0},... | collective-permute-start | bytes 1572872 | tf_op jit(solution)/shard_map/ppermute | solution.py:21
  81.8 0.2 collective-permute-start.7
  82.0 1.7 %convolution_subtract_fusion = f32[256,512]{1,0:T(8,128)S(1)} fusion(f32[256,512]{1,0:T(8,128)S(1)} %fusion.31, f32[512,512]{1,0:T(8,128)} %param.5, f32[512,256]{1,0:T(8,128)S(1)} %fusion.8), kind=kOutput, calls=%fused_computation | convolution fusion | flops 402784256 | bytes 1835008 | tf_op jit(solution)/shard_map/dot_general | solution.py:25
  83.7 31.3 %collective-permute-done.7 = f32[256,256]{1,0:T(8,128)S(1)} collective-permute-done((f32[256,256]{1,0:T(8,128)S(1)}, f32[256,256]{1,0:T(8,128)S(1)}, u32[]{:S(2)}, u32[]{:S(2)}) %collective-permute-start.7) | collective-permute-done | bytes 262176 | tf_op jit(solution)/shard_map/ppermute | solution.py:21
  115.0 0.0 collective-permute-done.8
  115.0 0.7 fusion.9
  115.7 0.7 fusion.3
  116.4 1.0 pad_maximum_fusion
  (1 shorter events, 0.0 us)
Async XLA Ops:
  0.0 19.2 %copy-start = (f32[512,512]{1,0:T(8,128)S(1)}, f32[512,512]{1,0:T(8,128)}, u32[]{:S(2)}) copy-start(f32[512,512]{1,0:T(8,128)} %param.5) | copy-start | bytes 3145732
  0.0 18.1 %collective-permute-start = (f32[512,128]{1,0:T(8,128)}, f32[512,128]{1,0:T(8,128)S(1)}, u32[]{:S(2)}, u32[]{:S(2)}) collective-permute-start(f32[512,128]{1,0:T(8,128)} %param.6), channel_id=1, source_target_pairs={{0,1},{1,0},{2,3},{3,2},{4,5},{5,4},{6,7},{7,6},{8,9},{9,8},{10,11... | collective-permute-start | bytes 786440 | tf_op jit(solution)/shard_map/ppermute | solution.py:14
  21.6 1.5 %copy-start.1 = (f32[256,128]{1,0:T(8,128)S(1)}, f32[256,128]{1,0:T(8,128)}, u32[]{:S(2)}) copy-start(f32[256,128]{1,0:T(8,128)} %param.9) | copy-start | bytes 393220
  23.1 8.5 %collective-permute-start.2 = (f32[256,512]{1,0:T(8,128)}, f32[256,512]{1,0:T(8,128)S(1)}, u32[]{:S(2)}, u32[]{:S(2)}) collective-permute-start(f32[256,512]{1,0:T(8,128)} %get-tuple-element.5), channel_id=1, source_target_pairs={{0,2},{2,0},{4,6},{6,4},{8,10},{10,8},{12,14},{14,12},{16,18},{18,... | collective-permute-start | bytes 1572872 | tf_op jit(solution)/shard_map/ppermute | solution.py:21
  30.0 1.6 %collective-permute-start.1 = (f32[256,256]{1,0:T(8,128)S(1)}, f32[256,256]{1,0:T(8,128)S(1)}, u32[]{:S(2)}, u32[]{:S(2)}) collective-permute-start(f32[256,256]{1,0:T(8,128)S(1)} %fusion.33), channel_id=1, source_target_pairs={{0,2},{2,0},{4,6},{6,4},{8,10},{10,8},{12,14},{14,12},{16,18},{18,... | collective-permute-start | bytes 786440 | tf_op jit(solution)/shard_map/ppermute | solution.py:21
  34.5 19.8 %collective-permute-start.4 = (f32[256,512]{1,0:T(8,128)}, f32[256,512]{1,0:T(8,128)S(1)}, u32[]{:S(2)}, u32[]{:S(2)}) collective-permute-start(f32[256,512]{1,0:T(8,128)} %get-tuple-element.7), channel_id=1, source_target_pairs={{0,4},{2,6},{4,0},{6,2},{8,12},{10,14},{12,8},{14,10},{16,20},{18,... | collective-permute-start | bytes 1572872 | tf_op jit(solution)/shard_map/ppermute | solution.py:21
  36.2 18.1 %collective-permute-start.3 = (f32[256,256]{1,0:T(8,128)S(1)}, f32[256,256]{1,0:T(8,128)S(1)}, u32[]{:S(2)}, u32[]{:S(2)}) collective-permute-start(f32[256,256]{1,0:T(8,128)S(1)} %fusion.33), channel_id=1, source_target_pairs={{0,4},{2,6},{4,0},{6,2},{8,12},{10,14},{12,8},{14,10},{16,20},{18,... | collective-permute-start | bytes 786440 | tf_op jit(solution)/shard_map/ppermute | solution.py:21
  57.2 19.0 %collective-permute-start.6 = (f32[256,512]{1,0:T(8,128)}, f32[256,512]{1,0:T(8,128)S(1)}, u32[]{:S(2)}, u32[]{:S(2)}) collective-permute-start(f32[256,512]{1,0:T(8,128)} %get-tuple-element.9), channel_id=1, source_target_pairs={{0,8},{2,10},{4,12},{6,14},{8,0},{10,2},{12,4},{14,6},{16,24},{18,... | collective-permute-start | bytes 1572872 | tf_op jit(solution)/shard_map/ppermute | solution.py:21
  59.0 17.2 %collective-permute-start.5 = (f32[256,256]{1,0:T(8,128)S(1)}, f32[256,256]{1,0:T(8,128)S(1)}, u32[]{:S(2)}, u32[]{:S(2)}) collective-permute-start(f32[256,256]{1,0:T(8,128)S(1)} %fusion.33), channel_id=1, source_target_pairs={{0,8},{2,10},{4,12},{6,14},{8,0},{10,2},{12,4},{14,6},{16,24},{18,... | collective-permute-start | bytes 786440 | tf_op jit(solution)/shard_map/ppermute | solution.py:21
  79.1 35.9 %collective-permute-start.8 = (f32[256,512]{1,0:T(8,128)}, f32[256,512]{1,0:T(8,128)S(1)}, u32[]{:S(2)}, u32[]{:S(2)}) collective-permute-start(f32[256,512]{1,0:T(8,128)} %get-tuple-element.11), channel_id=1, source_target_pairs={{0,16},{2,18},{4,20},{6,22},{8,24},{10,26},{12,28},{14,30},{16,0},... | collective-permute-start | bytes 1572872 | tf_op jit(solution)/shard_map/ppermute | solution.py:21
  81.8 33.2 %collective-permute-start.7 = (f32[256,256]{1,0:T(8,128)S(1)}, f32[256,256]{1,0:T(8,128)S(1)}, u32[]{:S(2)}, u32[]{:S(2)}) collective-permute-start(f32[256,256]{1,0:T(8,128)S(1)} %fusion.33), channel_id=1, source_target_pairs={{0,16},{2,18},{4,20},{6,22},{8,24},{10,26},{12,28},{14,30},{16,0},... | collective-permute-start | bytes 786440 | tf_op jit(solution)/shard_map/ppermute | solution.py:21
